TPU v7x, 256 devices: a whole 4x4x8 slice. The times are simulated.
256 devices in a mesh: cfg: 2 (over z_lo), seq: 16 (over z_hi, x), wblk: 8 (over y, core).
Axes of the slice: x: 4, y: 4, z: 8 (z_hi: 4, z_lo: 2; z = z_hi * 2 + z_lo), core: 2. Of those that a mesh axis runs over, the one named last changes fastest.
Arguments:
- text_tokens: bfloat16 [2, 2, 512, 3072], P('cfg', None, 'seq', 'wblk'), may hold values from -16 to 16
- image_tokens: bfloat16 [2, 4096, 3072], P(None, 'seq', 'wblk'), may hold values from -16 to 16
- pooled_vector: float32 [2, 3072], P('cfg', 'seq'), may hold values from -6 to 6
- mod_weight: bfloat16 [3072, 3, 3072], P('seq', None, 'wblk'), may hold values from -0.109375 to 0.109375
- qkv_weight: bfloat16 [3072, 3, 16, 128], P('seq', None, 'wblk'), may hold values from -0.109375 to 0.109375
- up_weight: bfloat16 [3072, 6144], P('seq', 'wblk'), may hold values from -0.109375 to 0.109375
- query_gain: float32 [128], replicated, may hold values from 0.6 to 10
- key_gain: float32 [128], replicated, may hold values from 0.6 to 10
- attn_weight: bfloat16 [2048, 3072], P('wblk', 'seq'), may hold values from -0.125 to 0.125
- down_weight: bfloat16 [6144, 3072], P('wblk', 'seq'), may hold values from -0.078125 to 0.078125
- lengths: int32 [2], replicated, may hold values from 1 to 512, as said below
- timestep: int32 [1], replicated, may hold values from 0 to 27
Outputs:
- text_out: bfloat16 [2, 2, 512, 3072], P('cfg', None, 'seq', 'wblk')
- velocity: float32 [2, 4096, 3072], P('cfg', 'seq', 'wblk')
- new_image: float32 [2, 4096, 3072], P('cfg', 'seq', 'wblk')
Inputs may be any that keep to these rules, and one draw needn't show every extreme that they name: `lengths`: some prompt has all 512 text tokens live in every draw.
All inputs are finite; a program needn't handle non-finite values.
Results may differ from a plain program's by a relative error of at most 0.025.
Values may be sent and summed in bfloat16 or wider, within the bound.
No kernel may reach another device: no remote copies, remote signals or barrier semaphores. Data moves between devices by JAX's collectives and lax.ppermute only.
A program may use at most 128 MiB of HBM per device.

v0:
```python
import math
import jax
import jax.numpy as jnp
from jax import lax
from jax.sharding import PartitionSpec as P

D = 3072
HD = 128
GRID = 64
STEPS = 28
epsilon = 1e-06
guidance = 3.5
time_shift = 3.0
rope_theta = 10000.0


def plan(timestep):
    step_index = timestep[0].astype(jnp.float32)
    time_now = 1.0 - step_index / STEPS
    time_next = 1.0 - (step_index + 1.0) / STEPS
    sigma_now = time_shift * time_now / (1.0 + (time_shift - 1.0) * time_now)
    sigma_next = time_shift * time_next / (1.0 + (time_shift - 1.0) * time_next)
    return (sigma_now, sigma_next - sigma_now)


def time_embedding(sigma_now, dim_count):
    halfwidth = dim_count // 2
    frequency = jnp.exp(-math.log(10000.0) * jnp.arange(halfwidth, dtype=jnp.float32) / halfwidth)
    angles = 1000.0 * sigma_now * frequency
    return jnp.concatenate([jnp.cos(angles), jnp.sin(angles)])


def inverse_freq(dim_count):
    return rope_theta ** (-jnp.arange(0, dim_count, 2, dtype=jnp.float32) / dim_count)


def rotary_angles(height_pos, width_pos):
    still_dims = HD // 8
    axis_dims = (HD - still_dims) // 2
    return jnp.concatenate(
        [
            jnp.zeros((height_pos.shape[0], still_dims // 2), jnp.float32),
            height_pos[:, None] * inverse_freq(axis_dims)[None],
            width_pos[:, None] * inverse_freq(axis_dims)[None],
        ],
        axis=1,
    )


def rotate(vectors, angles):
    paired_dims = vectors.reshape(vectors.shape[:-1] + (HD // 2, 2))
    cosine_table = jnp.cos(angles)[:, None, :]
    sine_table = jnp.sin(angles)[:, None, :]
    first_part = paired_dims[..., 0]
    second_part = paired_dims[..., 1]
    turned = jnp.stack(
        [
            first_part * cosine_table - second_part * sine_table,
            first_part * sine_table + second_part * cosine_table,
        ],
        axis=-1,
    )
    return turned.reshape(vectors.shape)


def head_norm(vectors, gain_vector):
    return (
        vectors
        * lax.rsqrt(jnp.mean(vectors * vectors, axis=-1, keepdims=True) + epsilon)
        * gain_vector
    )


def input_folder(source, pieces):
    width_rows = pieces[0].shape[0]
    first_total = jnp.dot(
        source, pieces[0].reshape(width_rows, -1), preferred_element_type=jnp.float32
    )
    second_total = jnp.dot(source, pieces[1], preferred_element_type=jnp.float32)
    return (first_total, second_total)


def output_folder(attended, activated, pieces):
    block_cols = jnp.dot(attended, pieces[0], preferred_element_type=jnp.float32)
    block_cols = block_cols + jnp.dot(activated, pieces[1], preferred_element_type=jnp.float32)
    return block_cols


def shards(
    text_tokens,
    image_tokens,
    pooled_vector,
    mod_weight,
    qkv_weight,
    up_weight,
    query_gain,
    key_gain,
    attn_weight,
    down_weight,
    lengths,
    timestep,
):
    seq_pos = lax.axis_index("seq")
    cfg_pos = lax.axis_index("cfg")
    prompts = image_tokens.shape[0]
    image_rows = image_tokens.shape[1]
    text_rows = text_tokens.shape[2]
    local_len = text_rows + image_rows
    dim_local = image_tokens.shape[2]
    dim_seq = pooled_vector.shape[1]
    heads_local = qkv_weight.shape[2]
    row_count = prompts * local_len
    sigma_now, step_size = plan(timestep)
    embedded = lax.dynamic_slice_in_dim(time_embedding(sigma_now, D), seq_pos * dim_seq, dim_seq)
    cond_vec = jax.nn.silu(pooled_vector[0] + embedded).astype(jnp.bfloat16)[None]
    mod_terms = jnp.dot(
        cond_vec, mod_weight.reshape(dim_seq, 3 * dim_local), preferred_element_type=jnp.float32
    )
    seq_count = lax.psum(1, "seq")
    mod_spread = jnp.broadcast_to(mod_terms.reshape(1, 3, dim_local), (seq_count, 3, dim_local))
    modulation = jnp.sum(lax.all_to_all(mod_spread, "seq", 0, 0, tiled=True), axis=0)
    local_rows = jnp.concatenate([text_tokens[0], image_tokens], axis=1)
    hidden = local_rows.astype(jnp.float32)
    totals, squares = lax.psum(
        (jnp.sum(hidden, axis=-1), jnp.sum(hidden * hidden, axis=-1)), "wblk"
    )
    average = (totals / D)[..., None]
    variance = (squares / D)[..., None] - average * average
    normed = (
        (hidden - average) * lax.rsqrt(variance + epsilon) * (1.0 + modulation[1]) + modulation[0]
    ).astype(jnp.bfloat16)
    width_rows = qkv_weight.shape[0]
    qkv_cols = 3 * heads_local * HD
    qkv_full = lax.all_gather(qkv_weight.reshape(width_rows, qkv_cols), "seq", axis=0, tiled=True)
    wblk_count = lax.psum(1, "wblk")
    spread = jnp.broadcast_to(
        normed.reshape(row_count, 1, dim_local), (row_count, wblk_count, dim_local)
    )
    gathered = lax.all_to_all(spread, "wblk", 1, 1, tiled=True).reshape(row_count, D)
    up_cols = up_weight.shape[1]
    tail_source = jnp.concatenate(
        [up_weight, jnp.concatenate([attn_weight, down_weight], axis=0).T], axis=1
    )
    tail_source, gathered = lax.optimization_barrier((tail_source, gathered))
    tail_full = lax.all_gather(tail_source, "seq", axis=0, tiled=True)
    up_full, out_weight_t = lax.optimization_barrier(
        (tail_full[:, :up_cols], tail_full[:, up_cols:])
    )
    projected = jnp.einsum("rk,kn->rn", gathered, qkv_full, preferred_element_type=jnp.float32)
    mlp_units = jnp.einsum("rk,kn->rn", gathered, up_full, preferred_element_type=jnp.float32)
    projected = projected.reshape(prompts, local_len, 3, heads_local, HD)
    image_index = seq_pos * image_rows + jnp.arange(image_rows, dtype=jnp.int32)
    height_pos = jnp.concatenate(
        [jnp.zeros((text_rows,), jnp.float32), (image_index // GRID).astype(jnp.float32)]
    )
    width_pos = jnp.concatenate(
        [jnp.zeros((text_rows,), jnp.float32), (image_index % GRID).astype(jnp.float32)]
    )
    angles = rotary_angles(height_pos, width_pos)
    queries = rotate(head_norm(projected[:, :, 0], query_gain), angles).astype(jnp.bfloat16)
    key_rows = rotate(head_norm(projected[:, :, 1], key_gain), angles).astype(jnp.bfloat16)
    values = projected[:, :, 2].astype(jnp.bfloat16)
    scale_factor = HD ** (-0.5)
    pair_count = prompts * heads_local
    subs = seq_count // pair_count
    sub_rows = local_len // subs
    pair_keys = key_rows.transpose(0, 2, 1, 3).reshape(pair_count, local_len, HD)
    pair_values = values.transpose(0, 2, 1, 3).reshape(pair_count, local_len, HD)
    pair_queries = queries.transpose(0, 2, 1, 3).reshape(seq_count, sub_rows, HD)
    send = jnp.concatenate(
        [
            jnp.broadcast_to(pair_keys[:, None], (pair_count, subs, local_len, HD)).reshape(
                seq_count, local_len, HD
            ),
            jnp.broadcast_to(pair_values[:, None], (pair_count, subs, local_len, HD)).reshape(
                seq_count, local_len, HD
            ),
            pair_queries,
        ],
        axis=1,
    )
    received = lax.all_to_all(send, "seq", 0, 0, tiled=True)
    key_piece = received[:, :local_len].reshape(seq_count * local_len, HD)
    value_piece = received[:, local_len : 2 * local_len].reshape(seq_count * local_len, HD)
    query_piece = received[:, 2 * local_len :].reshape(seq_count * sub_rows, HD)
    my_prompt = seq_pos // subs // heads_local
    width_keys = key_piece.shape[0]
    where_global = jnp.arange(width_keys, dtype=jnp.int32)
    shard_index = where_global // local_len
    within = where_global % local_len
    text_index = shard_index * text_rows + within
    key_live = (within >= text_rows) | (text_index < lengths[my_prompt])
    scores = jnp.dot(query_piece, key_piece.T, preferred_element_type=jnp.float32) * scale_factor
    scores = jnp.where(key_live[None, :], scores, -1e30)
    top_score = jnp.max(scores, axis=-1, keepdims=True)
    weights = jnp.exp(scores - top_score)
    denominator = jnp.sum(weights, axis=-1, keepdims=True)
    numerator = jnp.dot(
        weights.astype(jnp.bfloat16), value_piece, preferred_element_type=jnp.float32
    )
    mixed = (numerator / denominator).astype(jnp.bfloat16).reshape(seq_count, sub_rows, HD)
    returned = lax.all_to_all(mixed, "seq", 0, 0, tiled=True)
    attended = returned.reshape(prompts, heads_local, local_len, HD)
    attended = attended.transpose(0, 2, 1, 3).reshape(row_count, heads_local * HD)
    activated = jax.nn.gelu(mlp_units, approximate=True).astype(jnp.bfloat16)
    block_terms = jnp.einsum(
        "bjk,rk->brj",
        out_weight_t.reshape(wblk_count, dim_local, -1),
        jnp.concatenate([attended, activated], axis=1),
        preferred_element_type=jnp.float32,
    )
    branch = lax.psum_scatter(
        block_terms.astype(jnp.bfloat16), "wblk", scatter_dimension=0, tiled=True
    )
    branch = branch.reshape(prompts, local_len, dim_local).astype(jnp.float32)
    layer_out = hidden + modulation[2] * branch
    text_out = layer_out[:, :text_rows].astype(jnp.bfloat16)[None]
    image_out = layer_out[:, text_rows:]
    own_prompts = prompts // 2
    rounded_out = image_out.astype(jnp.bfloat16)
    kept = lax.dynamic_slice_in_dim(rounded_out, cfg_pos * own_prompts, own_prompts, 0)
    given = lax.dynamic_slice_in_dim(rounded_out, (1 - cfg_pos) * own_prompts, own_prompts, 0)
    taken = lax.ppermute(given, "cfg", [(0, 1), (1, 0)]).astype(jnp.float32)
    kept = kept.astype(jnp.float32)
    conditional = jnp.where(cfg_pos == 0, kept, taken)
    unconditional = jnp.where(cfg_pos == 0, taken, kept)
    velocity = unconditional + guidance * (conditional - unconditional)
    latent = lax.dynamic_slice_in_dim(image_tokens, cfg_pos * own_prompts, own_prompts, 0).astype(
        jnp.float32
    )
    new_image = latent + step_size * velocity
    return (text_out, velocity, new_image)


def solution(mesh):
    in_specs = (
        P("cfg", None, "seq", "wblk"),
        P(None, "seq", "wblk"),
        P("cfg", "seq"),
        P("seq", None, "wblk"),
        P("seq", None, "wblk", None),
        P("seq", "wblk"),
        P(),
        P(),
        P("wblk", "seq"),
        P("wblk", "seq"),
        P(),
        P(),
    )
    out_specs = (P("cfg", None, "seq", "wblk"), P("cfg", "seq", "wblk"), P("cfg", "seq", "wblk"))
    return jax.shard_map(shards, mesh=mesh, in_specs=in_specs, out_specs=out_specs, check_vma=False)
```

profile of v0, /device:TPU:2, one launch (start us, length us, event | category | flops | bytes accessed | tf_op | source)
XLA Modules:
  0.0 356.4 jit_solution(5952095517683835310)
XLA Ops:
  7.2 1.9 reshape.270
  9.8 0.1 fusion.46
  9.9 0.8 fusion.54
  10.7 0.2 fusion.28
  10.9 0.7 broadcast_in_dim.24
  11.6 11.5 %all-to-all-start = ((f32[16,3,384]{2,1,0:T(4,128)}), f32[16,3,384]{2,1,0:T(4,128)S(1)}, u32[]{:S(2)}, u32[]{:S(2)}) async-start(f32[16,3,384]{2,1,0:T(4,128)} %broadcast_in_dim.24), calls=%async_computation | async-start | bytes 196608 | tf_op jit(solution)/shard_map/all_to_all | solution.py:121
  23.0 1.3 convert_reduce_fusion
  24.3 14.8 %all-reduce.2 = (f32[2,288]{1,0:T(2,128)S(1)}, f32[2,288]{1,0:T(2,128)S(1)}) all-reduce(f32[2,288]{1,0:T(2,128)S(1)} %get-tuple-element.12, f32[2,288]{1,0:T(2,128)S(1)} %get-tuple-element.11), channel_id=1, replica_groups=mesh['cfg'=2,'seq'=16,'wblk'=8] {'wblk'}, use_global_device_ids=true, to_apply=%region_4.5 | all-reduce | flops 1152 | bytes 9216 | tf_op jit(solution)/shard_map/psum | solution.py:124
  39.2 0.1 mul.288
  39.3 0.1 sub.76
  39.4 1.0 fusion.27
  40.5 2.1 broadcast_in_dim.26
  42.6 4.6 %all-to-all-start.1 = ((bf16[576,8,384]{2,0,1:T(8,128)(2,1)}), bf16[576,8,384]{2,0,1:T(8,128)(2,1)}, u32[]{:S(2)}, u32[]{:S(2)}) async-start(bf16[576,8,384]{2,0,1:T(8,128)(2,1)} %broadcast_in_dim.26), calls=%async_computation.1 | async-start | bytes 7077888 | tf_op jit(solution)/shard_map/all_to_all | solution.py:139
  47.2 0.0 all-gather.5.cloned.1.call-start
  47.4 0.9 pad_maximum_fusion.1
  48.3 41.6 %all-to-all-done.1 = bf16[576,8,384]{2,0,1:T(8,128)(2,1)} async-done(((bf16[576,8,384]{2,0,1:T(8,128)(2,1)}), bf16[576,8,384]{2,0,1:T(8,128)(2,1)}, u32[]{:S(2)}, u32[]{:S(2)}) %all-to-all-start.1) | async-done | bytes 3538976 | tf_op jit(solution)/shard_map/all_to_all | solution.py:139
  89.9 4.4 %copy.66 = bf16[8,72,8,384]{3,2,0,1:T(8,128)(2,1)} copy(bf16[8,72,8,384]{3,2,1,0:T(8,128)(2,1)} %bitcast.42) | data formatting | bytes 7077888 | tf_op jit(solution)/shard_map/reshape | solution.py:139
  94.3 0.1 mul.315
  94.5 0.1 mul.296
  94.7 0.1 concatenate.39
  94.7 0.1 concatenate.40
  94.8 0.1 broadcast_multiply_fusion.1
  94.9 0.4 fusion.35
  95.3 7.6 %fusion.60 = f32[576,768]{1,0:T(8,128)} fusion(bf16[576,3072]{1,0:T(8,128)(2,1)} %bitcast.91, bf16[3072,768]{1,0:T(8,128)(2,1)} %all-gather.3.cloned.1.call-done), kind=kOutput, calls=%fused_computation.113 | convolution fusion | flops 2717908992 | bytes 10027008 | tf_op jit(solution)/shard_map/rk,kn->rn/dot_general | solution.py:149
  102.9 2.2 reshape.271
  105.1 0.2 slice.77
  105.3 1.2 fusion.58
  106.5 1.4 copy.62
  107.9 0.5 copy.61
  108.4 0.4 multiply_reduce_fusion.1
  108.8 0.4 multiply_reduce_fusion.2
  109.2 0.4 multiply_multiply_fusion.1
  109.5 0.4 multiply_multiply_fusion.2
  109.9 0.8 subtract_convert_fusion.1
  110.7 0.6 pad_maximum_fusion.3
  111.3 0.5 copy.50
  111.8 0.6 pad_maximum_fusion.4
  112.4 0.5 copy.53
  112.9 0.2 broadcast_in_dim.29
  113.1 0.2 broadcast_in_dim.35
  113.3 1.7 pad_maximum_fusion
  115.0 10.0 %all-to-all-start.2 = ((bf16[16,648,128]{2,1,0:T(8,128)(2,1)}), bf16[16,648,128]{2,1,0:T(8,128)(2,1)S(1)}, u32[]{:S(2)}, u32[]{:S(2)}) async-start(bf16[16,648,128]{2,1,0:T(8,128)(2,1)} %pad_maximum_fusion), calls=%async_computation.2 | async-start | bytes 5308416 | tf_op jit(solution)/shard_map/all_to_all | solution.py:182
  125.0 0.2 reduce-scatter.2.cloned.1.call-start
  125.2 0.6 dynamic_slice.16
  125.8 0.7 fusion.45
  126.5 82.2 %all-to-all-done.2 = bf16[16,648,128]{2,1,0:T(8,128)(2,1)S(1)} async-done(((bf16[16,648,128]{2,1,0:T(8,128)(2,1)}), bf16[16,648,128]{2,1,0:T(8,128)(2,1)S(1)}, u32[]{:S(2)}, u32[]{:S(2)}) %all-to-all-start.2) | async-done | bytes 2654240 | tf_op jit(solution)/shard_map/all_to_all | solution.py:182
  208.7 0.2 fusion.57
  208.9 3.5 fusion.59
  212.4 4.2 %fusion.1 = f32[1152]{0:T(1024)S(1)} fusion(f32[1152,4608]{1,0:T(8,128)S(1)} %get-tuple-element.37, f32[1152]{0:T(1024)S(1)} %get-tuple-element.36), kind=kLoop, calls=%fused_computation.3 | loop fusion | flops 10615680 | bytes 21242880 | tf_op jit(solution)/shard_map/reduce_sum | solution.py:197
  216.6 3.2 copy-done.2
  219.9 10.6 %fusion.9 = bf16[1152,128]{1,0:T(8,128)(2,1)S(1)} fusion(bf16[4608,128]{1,0:T(8,128)(2,1)S(1)} %bitcast.87, f32[1152,4608]{1,0:T(8,128)} %copy-done.2, f32[1152]{0:T(1024)S(1)} %get-tuple-element.36, f32[1152]{0:T(1024)S(1)} %fusion.1), kind=kOutput, calls=%fused_computation.11 | convolution fusion | flops 1369866240 | bytes 22717440 | tf_op jit(solution)/shard_map/dot_general | solution.py:198
  230.4 28.2 %all_to_all.20 = bf16[16,72,128]{2,1,0:T(8,128)(2,1)S(1)} all-to-all(bf16[16,72,128]{2,1,0:T(8,128)(2,1)S(1)} %bitcast.94), channel_id=1, replica_groups=mesh['cfg'=2,'seq'=16,'wblk'=8] {'seq'}, dimensions={0} | all-to-all | bytes 589824 | tf_op jit(solution)/shard_map/all_to_all | solution.py:202
  258.6 0.2 copy.54
  258.9 31.0 %all-gather.5.cloned.1.call-done = bf16[3072,1792]{1,0:T(8,128)(2,1)} async-done(((bf16[192,1792]{1,0:T(8,128)(2,1)}), bf16[3072,1792]{1,0:T(8,128)(2,1)}) %all-gather.5.cloned.1.call-update) | async-done | bytes 11010064 | tf_op jit(solution)/shard_map/all_gather | solution.py:145
  289.8 2.3 slice-done.1
  292.2 1.1 copy-done.4
  293.3 3.1 fusion.19
  296.4 5.4 %convert_bitcast_fusion = bf16[8,576,384]{2,1,0:T(8,128)(2,1)} fusion(bf16[8,384,1024]{2,1,0:T(8,128)(2,1)S(1)} %bitcast.84, bf16[576,768]{1,0:T(8,128)(2,1)S(1)} %fusion.19, bf16[576,256]{1,0:T(8,128)(2,1)S(1)} %bitcast.106), kind=kOutput, calls=%fused_computation.7 | convolution fusion | flops 3628007424 | bytes 11010048 | tf_op jit(solution)/shard_map/bjk,rk->brj/dot_general | solution.py:206
  301.9 40.0 %reduce-scatter.2.cloned.1.call-done = bf16[1,576,384]{2,1,0:T(8,128)(2,1)} async-done(((bf16[8,576,384]{2,1,0:T(8,128)(2,1)}), bf16[1,576,384]{2,1,0:T(8,128)(2,1)}) %reduce-scatter.2.cloned.1.call-update) | async-done | bytes 442384 | tf_op jit(solution)/shard_map/reduce_scatter | solution.py:212
  341.9 1.1 fusion.23
  343.1 1.5 collective-permute-start
  344.7 0.6 slice_bitcast_fusion
  345.3 3.6 %collective-permute-done = bf16[1,256,384]{2,1,0:T(8,128)(2,1)S(1)} collective-permute-done((bf16[1,256,384]{2,1,0:T(8,128)(2,1)S(1)}, bf16[1,256,384]{2,1,0:T(8,128)(2,1)S(1)}, u32[]{:S(2)}, u32[]{:S(2)}) %collective-permute-start) | collective-permute-done | bytes 196640 | tf_op jit(solution)/shard_map/ppermute | solution.py:223
  348.9 1.0 multiply_add_fusion
  (48 shorter events, 0.5 us)
Async XLA Ops:
  7.2 3.5 copy-start
  7.2 32.2 %copy-start.3 = (bf16[2,256,384]{2,1,0:T(8,128)(2,1)S(1)}, bf16[2,256,384]{2,1,0:T(8,128)(2,1)}, u32[]{:S(2)}) copy-start(bf16[2,256,384]{2,1,0:T(8,128)(2,1)} %param.13) | copy-start | bytes 1179652
  7.2 88.1 %all-gather.3.cloned.1.call-start = ((), (), s32[]{:S(2)}) async-start(), calls=%async_computation.5 | async-start | bytes 5013504 | tf_op jit(solution)/shard_map/all_gather | solution.py:134
  11.6 27.8 %all-to-all-start = ((f32[16,3,384]{2,1,0:T(4,128)}), f32[16,3,384]{2,1,0:T(4,128)S(1)}, u32[]{:S(2)}, u32[]{:S(2)}) async-start(f32[16,3,384]{2,1,0:T(4,128)} %broadcast_in_dim.24), calls=%async_computation | async-start | bytes 196608 | tf_op jit(solution)/shard_map/all_to_all | solution.py:121
  42.6 4.7 %copy-start.6 = (bf16[768,192]{0,1:T(8,128)(2,1)S(1)}, bf16[768,192]{0,1:T(8,128)(2,1)}, u32[]{:S(2)}) copy-start(bf16[768,192]{0,1:T(8,128)(2,1)} %param.21) | copy-start | bytes 884740
  42.6 4.7 %copy-start.8 = (bf16[256,192]{0,1:T(8,128)(2,1)S(1)}, bf16[256,192]{0,1:T(8,128)(2,1)}, u32[]{:S(2)}) copy-start(bf16[256,192]{0,1:T(8,128)(2,1)} %param.20) | copy-start | bytes 294916
  42.6 4.8 %copy-start.7 = (bf16[192,768]{1,0:T(8,128)(2,1)S(1)}, bf16[192,768]{1,0:T(8,128)(2,1)}, u32[]{:S(2)}) copy-start(bf16[192,768]{1,0:T(8,128)(2,1)} %param.17) | copy-start | bytes 884740
  42.6 47.3 %all-to-all-start.1 = ((bf16[576,8,384]{2,0,1:T(8,128)(2,1)}), bf16[576,8,384]{2,0,1:T(8,128)(2,1)}, u32[]{:S(2)}, u32[]{:S(2)}) async-start(bf16[576,8,384]{2,0,1:T(8,128)(2,1)} %broadcast_in_dim.26), calls=%async_computation.1 | async-start | bytes 7077888 | tf_op jit(solution)/shard_map/all_to_all | solution.py:139
  47.2 242.6 %all-gather.5.cloned.1.call-start = ((), (), s32[]{:S(2)}) async-start(), calls=%async_computation.6 | async-start | bytes 11698176 | tf_op jit(solution)/shard_map/all_gather | solution.py:145
  89.9 4.5 %copy-start.9 = (f32[128]{0:T(128)S(1)}, f32[128]{0:T(128)}, u32[]{:S(2)}) copy-start(f32[128]{0:T(128)} %param.18) | copy-start | bytes 1540
  89.9 4.6 %copy-start.10 = (f32[128]{0:T(128)S(1)}, f32[128]{0:T(128)}, u32[]{:S(2)}) copy-start(f32[128]{0:T(128)} %param.19) | copy-start | bytes 1540
  115.0 10.3 %copy-start.11 = (s32[2]{0:T(128)S(1)}, s32[2]{0:T(128)}, u32[]{:S(2)}) copy-start(s32[2]{0:T(128)} %param.22) | copy-start | bytes 28
  115.0 93.7 %all-to-all-start.2 = ((bf16[16,648,128]{2,1,0:T(8,128)(2,1)}), bf16[16,648,128]{2,1,0:T(8,128)(2,1)S(1)}, u32[]{:S(2)}, u32[]{:S(2)}) async-start(bf16[16,648,128]{2,1,0:T(8,128)(2,1)} %pad_maximum_fusion), calls=%async_computation.2 | async-start | bytes 5308416 | tf_op jit(solution)/shard_map/all_to_all | solution.py:182
  125.0 216.9 %reduce-scatter.2.cloned.1.call-start = ((), (), s32[]{:S(2)}) async-start(), calls=%async_computation.7 | async-start | bytes 3981312 | tf_op jit(solution)/shard_map/reduce_scatter | solution.py:212
  212.4 7.5 %copy-start.2 = (f32[1152,4608]{1,0:T(8,128)}, f32[1152,4608]{1,0:T(8,128)S(1)}, u32[]{:S(2)}) copy-start(f32[1152,4608]{1,0:T(8,128)S(1)} %get-tuple-element.37) | copy-start | bytes 63700996
  289.8 2.3 slice-start.1
  289.8 3.5 copy-start.4
  293.3 3.1 slice-start
  301.8 40.1 %copy-start.5 = (bf16[1,2,32,384]{3,2,1,0:T(8,128)(2,1)S(1)}, bf16[1,2,32,384]{3,2,1,0:T(8,128)(2,1)}, u32[]{:S(2)}) copy-start(bf16[1,2,32,384]{3,2,1,0:T(8,128)(2,1)} %param.12) | copy-start | bytes 147460
  301.8 48.1 %copy-start.1 = (bf16[192,3,384]{2,0,1:T(8,128)(2,1)S(1)}, bf16[192,3,384]{2,0,1:T(8,128)(2,1)}, u32[]{:S(2)}) copy-start(bf16[192,3,384]{2,0,1:T(8,128)(2,1)} %param.15) | copy-start | bytes 1327108
  343.1 5.8 %collective-permute-start = (bf16[1,256,384]{2,1,0:T(8,128)(2,1)S(1)}, bf16[1,256,384]{2,1,0:T(8,128)(2,1)S(1)}, u32[]{:S(2)}, u32[]{:S(2)}) collective-permute-start(bf16[1,256,384]{2,1,0:T(8,128)(2,1)S(1)} %constant_dynamic-slice_fusion), channel_id=1, source_target_pairs={{0,128},{128,0},{1,129},{129,1},{2,130},{130,2},{3,131},{131,3},{4... | collective-permute-start | bytes 589832 | tf_op jit(solution)/shard_map/ppermute | solution.py:223
Sparse Core Ops, SparseCore 0:
  11.0 81.1 all-gather.2
  94.6 195.1 all-gather.4
  301.9 39.9 reduce-scatter.1
where the time goes:
time: 357 us; the launch traced here: 356 us
  waiting for transfers between devices  198 us (55%)
  blocking collectives  43 us (12%)
  matrix products  30.3 us (8%)
  starting transfers between devices  28 us (8%)
  local copies, waits for them, and re-layouts  25 us (7%)
  other arithmetic  16.8 us (5%)
  between operations  14.9 us (4%)
    all_to_all x1, waiting for transfers between devices, shards(): received = lax.all_to_all(send, 'seq', 0, 0, tiled=True)  82.2 us
    all_to_all x1, waiting for transfers between devices, shards(): lax.all_to_all(spread, 'wblk', 1, 1, tiled=True).reshape(row_count, D)  41.6 us
    reduce_scatter x1, waiting for transfers between devices, shards(): lax.psum_scatter(block_terms.astype(jnp.bfloat16), 'wblk', scatter_dimens...  40 us
    all_gather x1, waiting for transfers between devices, shards(): tail_full = lax.all_gather(tail_source, 'seq', axis=0, tiled=True)  31 us
    all_to_all x1, blocking collectives, shards(): returned = lax.all_to_all(mixed, 'seq', 0, 0, tiled=True)  28.2 us
    psum x1, blocking collectives, shards(): lax.psum((jnp.sum(hidden, axis=-1), jnp.sum(hidden * hidden, axis=-1)), '...  14.8 us
    all_to_all x1, starting transfers between devices, shards(): lax.all_to_all(mod_spread, 'seq', 0, 0, tiled=True)  11.5 us
    dot_general x1, matrix products, shards(): jnp.dot(weights.astype(jnp.bfloat16), value_piece, preferred_element_type...  10.6 us
  transfers between devices with their start and end apart: 7, of which 5 were waited for; matrix products, arithmetic and copies ran while one was open for 15% of the time, Pallas kernels for 0%

commit v1 on v0

--- a/solution.py
+++ b/solution.py
@@ -136,7 +136,10 @@
     spread = jnp.broadcast_to(
         normed.reshape(row_count, 1, dim_local), (row_count, wblk_count, dim_local)
     )
-    gathered = lax.all_to_all(spread, "wblk", 1, 1, tiled=True).reshape(row_count, D)
+    gathered = jnp.concatenate(
+        lax.all_to_all(jnp.stack(jnp.split(spread, lax.axis_size("wblk"), axis=1)), "wblk", 0, 0),
+        axis=1,
+    ).reshape(row_count, D)
     up_cols = up_weight.shape[1]
     tail_source = jnp.concatenate(
         [up_weight, jnp.concatenate([attn_weight, down_weight], axis=0).T], axis=1

time: 357 us -> 357 us (level)
    reshape x1 -> x0, local copies, waits for them, and re-layouts: 4.44 us -> none  [shards(): lax.all_to_all(spread, 'wblk', 1, 1, tiled=True).reshape(row_count, D)]
    unnamed x28 -> x29, local copies, waits for them, and re-layouts: 6.38 us -> 10.8 us
where the time goes in v1:
time: 357 us; the launch traced here: 356 us
  waiting for transfers between devices  198 us (55%)
  blocking collectives  43 us (12%)
  matrix products  30.3 us (8%)
  starting transfers between devices  28 us (8%)
  local copies, waits for them, and re-layouts  25 us (7%)
  other arithmetic  16.8 us (5%)
  between operations  14.9 us (4%)
    all_to_all x1, waiting for transfers between devices, shards(): received = lax.all_to_all(send, 'seq', 0, 0, tiled=True)  82.2 us
    all_to_all x1, waiting for transfers between devices, shards(): lax.all_to_all(jnp.stack(jnp.split(spread, lax.axis_size('wblk'), axis=1)...  41.6 us
    reduce_scatter x1, waiting for transfers between devices, shards(): lax.psum_scatter(block_terms.astype(jnp.bfloat16), 'wblk', scatter_dimens...  40 us
    all_gather x1, waiting for transfers between devices, shards(): tail_full = lax.all_gather(tail_source, 'seq', axis=0, tiled=True)  31 us
    all_to_all x1, blocking collectives, shards(): returned = lax.all_to_all(mixed, 'seq', 0, 0, tiled=True)  28.2 us
    psum x1, blocking collectives, shards(): lax.psum((jnp.sum(hidden, axis=-1), jnp.sum(hidden * hidden, axis=-1)), '...  14.8 us
    all_to_all x1, starting transfers between devices, shards(): lax.all_to_all(mod_spread, 'seq', 0, 0, tiled=True)  11.5 us
    unnamed x29, local copies, waits for them, and re-layouts  10.8 us
  transfers between devices with their start and end apart: 7, of which 5 were waited for; matrix products, arithmetic and copies ran while one was open for 15% of the time, Pallas kernels for 0%

profile of v1, /device:TPU:2, one launch (start us, length us, event | category | flops | bytes accessed | tf_op | source)
XLA Modules:
  0.0 356.4 jit_solution(5952095517683835310)
XLA Ops:
  7.2 1.9 reshape.330
  9.8 0.1 fusion.46
  9.9 0.8 fusion.54
  10.7 0.2 fusion.28
  10.9 0.7 broadcast_in_dim.22
  11.6 11.5 %all-to-all-start = ((f32[16,3,384]{2,1,0:T(4,128)}), f32[16,3,384]{2,1,0:T(4,128)S(1)}, u32[]{:S(2)}, u32[]{:S(2)}) async-start(f32[16,3,384]{2,1,0:T(4,128)} %broadcast_in_dim.22), calls=%async_computation | async-start | bytes 196608 | tf_op jit(solution)/shard_map/all_to_all | solution.py:121
  23.0 1.3 convert_reduce_fusion
  24.3 14.8 %all-reduce.2 = (f32[2,288]{1,0:T(2,128)S(1)}, f32[2,288]{1,0:T(2,128)S(1)}) all-reduce(f32[2,288]{1,0:T(2,128)S(1)} %get-tuple-element.12, f32[2,288]{1,0:T(2,128)S(1)} %get-tuple-element.11), channel_id=1, replica_groups=mesh['cfg'=2,'seq'=16,'wblk'=8] {'wblk'}, use_global_device_ids=true, to_apply=%region_4.5 | all-reduce | flops 1152 | bytes 9216 | tf_op jit(solution)/shard_map/psum | solution.py:124
  39.2 0.1 mul.296
  39.3 0.1 sub.80
  39.4 1.0 fusion.27
  40.5 2.1 stack.8
  42.6 4.6 %all-to-all-start.1 = ((bf16[8,576,1,384]{3,1,2,0:T(8,128)(2,1)}), bf16[8,576,1,384]{3,1,2,0:T(8,128)(2,1)}, u32[]{:S(2)}, u32[]{:S(2)}) async-start(bf16[8,576,1,384]{3,1,2,0:T(8,128)(2,1)} %stack.8), calls=%async_computation.1 | async-start | bytes 7077888 | tf_op jit(solution)/shard_map/all_to_all | solution.py:140
  47.2 0.0 all-gather.5.cloned.1.call-start
  47.4 0.9 pad_maximum_fusion.1
  48.3 41.6 %all-to-all-done.1 = bf16[8,576,1,384]{3,1,2,0:T(8,128)(2,1)} async-done(((bf16[8,576,1,384]{3,1,2,0:T(8,128)(2,1)}), bf16[8,576,1,384]{3,1,2,0:T(8,128)(2,1)}, u32[]{:S(2)}, u32[]{:S(2)}) %all-to-all-start.1) | async-done | bytes 3538976 | tf_op jit(solution)/shard_map/all_to_all | solution.py:140
  89.9 4.4 %copy.59 = bf16[72,8,8,384]{3,1,2,0:T(8,128)(2,1)} copy(bf16[72,8,8,384]{3,1,0,2:T(8,128)(2,1)} %bitcast.69) | data formatting | bytes 7077888
  94.3 0.1 mul.323
  94.5 0.1 mul.304
  94.7 0.1 concatenate.39
  94.7 0.1 concatenate.40
  94.8 0.1 broadcast_multiply_fusion.1
  94.9 0.4 fusion.35
  95.3 7.6 %fusion.60 = f32[576,768]{1,0:T(8,128)} fusion(bf16[576,3072]{1,0:T(8,128)(2,1)} %bitcast.96, bf16[3072,768]{1,0:T(8,128)(2,1)} %all-gather.3.cloned.1.call-done), kind=kOutput, calls=%fused_computation.113 | convolution fusion | flops 2717908992 | bytes 10027008 | tf_op jit(solution)/shard_map/rk,kn->rn/dot_general | solution.py:152
  102.9 2.2 reshape.331
  105.1 0.2 slice.77
  105.3 1.2 fusion.58
  106.5 1.4 copy.55
  107.9 0.5 copy.54
  108.4 0.4 multiply_reduce_fusion.1
  108.8 0.4 multiply_reduce_fusion.2
  109.2 0.4 multiply_multiply_fusion.1
  109.5 0.4 multiply_multiply_fusion.2
  109.9 0.8 subtract_convert_fusion.1
  110.7 0.6 pad_maximum_fusion.3
  111.3 0.5 copy.43
  111.8 0.6 pad_maximum_fusion.4
  112.4 0.5 copy.46
  112.9 0.2 broadcast_in_dim.26
  113.1 0.2 broadcast_in_dim.28
  113.3 1.7 pad_maximum_fusion
  115.0 10.0 %all-to-all-start.2 = ((bf16[16,648,128]{2,1,0:T(8,128)(2,1)}), bf16[16,648,128]{2,1,0:T(8,128)(2,1)S(1)}, u32[]{:S(2)}, u32[]{:S(2)}) async-start(bf16[16,648,128]{2,1,0:T(8,128)(2,1)} %pad_maximum_fusion), calls=%async_computation.2 | async-start | bytes 5308416 | tf_op jit(solution)/shard_map/all_to_all | solution.py:185
  125.0 0.2 reduce-scatter.2.cloned.1.call-start
  125.2 0.6 dynamic_slice.16
  125.8 0.7 fusion.45
  126.5 82.2 %all-to-all-done.2 = bf16[16,648,128]{2,1,0:T(8,128)(2,1)S(1)} async-done(((bf16[16,648,128]{2,1,0:T(8,128)(2,1)}), bf16[16,648,128]{2,1,0:T(8,128)(2,1)S(1)}, u32[]{:S(2)}, u32[]{:S(2)}) %all-to-all-start.2) | async-done | bytes 2654240 | tf_op jit(solution)/shard_map/all_to_all | solution.py:185
  208.7 0.2 fusion.57
  208.9 3.5 fusion.59
  212.4 4.2 %fusion.1 = f32[1152]{0:T(1024)S(1)} fusion(f32[1152,4608]{1,0:T(8,128)S(1)} %get-tuple-element.37, f32[1152]{0:T(1024)S(1)} %get-tuple-element.36), kind=kLoop, calls=%fused_computation.3 | loop fusion | flops 10615680 | bytes 21242880 | tf_op jit(solution)/shard_map/reduce_sum | solution.py:200
  216.6 3.2 copy-done.2
  219.9 10.6 %fusion.9 = bf16[1152,128]{1,0:T(8,128)(2,1)S(1)} fusion(bf16[4608,128]{1,0:T(8,128)(2,1)S(1)} %bitcast.92, f32[1152,4608]{1,0:T(8,128)} %copy-done.2, f32[1152]{0:T(1024)S(1)} %get-tuple-element.36, f32[1152]{0:T(1024)S(1)} %fusion.1), kind=kOutput, calls=%fused_computation.11 | convolution fusion | flops 1369866240 | bytes 22717440 | tf_op jit(solution)/shard_map/dot_general | solution.py:201
  230.4 28.2 %all_to_all.20 = bf16[16,72,128]{2,1,0:T(8,128)(2,1)S(1)} all-to-all(bf16[16,72,128]{2,1,0:T(8,128)(2,1)S(1)} %bitcast.99), channel_id=1, replica_groups=mesh['cfg'=2,'seq'=16,'wblk'=8] {'seq'}, dimensions={0} | all-to-all | bytes 589824 | tf_op jit(solution)/shard_map/all_to_all | solution.py:205
  258.6 0.2 copy.47
  258.9 31.0 %all-gather.5.cloned.1.call-done = bf16[3072,1792]{1,0:T(8,128)(2,1)} async-done(((bf16[192,1792]{1,0:T(8,128)(2,1)}), bf16[3072,1792]{1,0:T(8,128)(2,1)}) %all-gather.5.cloned.1.call-update) | async-done | bytes 11010064 | tf_op jit(solution)/shard_map/all_gather | solution.py:148
  289.8 2.3 slice-done.1
  292.2 1.1 copy-done.4
  293.3 3.1 fusion.19
  296.4 5.4 %convert_bitcast_fusion = bf16[8,576,384]{2,1,0:T(8,128)(2,1)} fusion(bf16[8,384,1024]{2,1,0:T(8,128)(2,1)S(1)} %bitcast.89, bf16[576,768]{1,0:T(8,128)(2,1)S(1)} %fusion.19, bf16[576,256]{1,0:T(8,128)(2,1)S(1)} %bitcast.111), kind=kOutput, calls=%fused_computation.7 | convolution fusion | flops 3628007424 | bytes 11010048 | tf_op jit(solution)/shard_map/bjk,rk->brj/dot_general | solution.py:209
  301.9 40.0 %reduce-scatter.2.cloned.1.call-done = bf16[1,576,384]{2,1,0:T(8,128)(2,1)} async-done(((bf16[8,576,384]{2,1,0:T(8,128)(2,1)}), bf16[1,576,384]{2,1,0:T(8,128)(2,1)}) %reduce-scatter.2.cloned.1.call-update) | async-done | bytes 442384 | tf_op jit(solution)/shard_map/reduce_scatter | solution.py:215
  341.9 1.1 fusion.23
  343.1 1.5 collective-permute-start
  344.7 0.6 slice_bitcast_fusion
  345.3 3.6 %collective-permute-done = bf16[1,256,384]{2,1,0:T(8,128)(2,1)S(1)} collective-permute-done((bf16[1,256,384]{2,1,0:T(8,128)(2,1)S(1)}, bf16[1,256,384]{2,1,0:T(8,128)(2,1)S(1)}, u32[]{:S(2)}, u32[]{:S(2)}) %collective-permute-start) | collective-permute-done | bytes 196640 | tf_op jit(solution)/shard_map/ppermute | solution.py:226
  348.9 1.0 multiply_add_fusion
  (48 shorter events, 0.5 us)
Async XLA Ops:
  7.2 3.5 copy-start
  7.2 32.2 %copy-start.3 = (bf16[2,256,384]{2,1,0:T(8,128)(2,1)S(1)}, bf16[2,256,384]{2,1,0:T(8,128)(2,1)}, u32[]{:S(2)}) copy-start(bf16[2,256,384]{2,1,0:T(8,128)(2,1)} %param.13) | copy-start | bytes 1179652
  7.2 88.1 %all-gather.3.cloned.1.call-start = ((), (), s32[]{:S(2)}) async-start(), calls=%async_computation.5 | async-start | bytes 5013504 | tf_op jit(solution)/shard_map/all_gather | solution.py:134
  11.6 27.8 %all-to-all-start = ((f32[16,3,384]{2,1,0:T(4,128)}), f32[16,3,384]{2,1,0:T(4,128)S(1)}, u32[]{:S(2)}, u32[]{:S(2)}) async-start(f32[16,3,384]{2,1,0:T(4,128)} %broadcast_in_dim.22), calls=%async_computation | async-start | bytes 196608 | tf_op jit(solution)/shard_map/all_to_all | solution.py:121
  42.6 4.7 %copy-start.6 = (bf16[768,192]{0,1:T(8,128)(2,1)S(1)}, bf16[768,192]{0,1:T(8,128)(2,1)}, u32[]{:S(2)}) copy-start(bf16[768,192]{0,1:T(8,128)(2,1)} %param.21) | copy-start | bytes 884740
  42.6 4.7 %copy-start.8 = (bf16[256,192]{0,1:T(8,128)(2,1)S(1)}, bf16[256,192]{0,1:T(8,128)(2,1)}, u32[]{:S(2)}) copy-start(bf16[256,192]{0,1:T(8,128)(2,1)} %param.20) | copy-start | bytes 294916
  42.6 4.8 %copy-start.7 = (bf16[192,768]{1,0:T(8,128)(2,1)S(1)}, bf16[192,768]{1,0:T(8,128)(2,1)}, u32[]{:S(2)}) copy-start(bf16[192,768]{1,0:T(8,128)(2,1)} %param.17) | copy-start | bytes 884740
  42.6 47.3 %all-to-all-start.1 = ((bf16[8,576,1,384]{3,1,2,0:T(8,128)(2,1)}), bf16[8,576,1,384]{3,1,2,0:T(8,128)(2,1)}, u32[]{:S(2)}, u32[]{:S(2)}) async-start(bf16[8,576,1,384]{3,1,2,0:T(8,128)(2,1)} %stack.8), calls=%async_computation.1 | async-start | bytes 7077888 | tf_op jit(solution)/shard_map/all_to_all | solution.py:140
  47.2 242.6 %all-gather.5.cloned.1.call-start = ((), (), s32[]{:S(2)}) async-start(), calls=%async_computation.6 | async-start | bytes 11698176 | tf_op jit(solution)/shard_map/all_gather | solution.py:148
  89.9 4.5 %copy-start.9 = (f32[128]{0:T(128)S(1)}, f32[128]{0:T(128)}, u32[]{:S(2)}) copy-start(f32[128]{0:T(128)} %param.18) | copy-start | bytes 1540
  89.9 4.6 %copy-start.10 = (f32[128]{0:T(128)S(1)}, f32[128]{0:T(128)}, u32[]{:S(2)}) copy-start(f32[128]{0:T(128)} %param.19) | copy-start | bytes 1540
  115.0 10.3 %copy-start.11 = (s32[2]{0:T(128)S(1)}, s32[2]{0:T(128)}, u32[]{:S(2)}) copy-start(s32[2]{0:T(128)} %param.22) | copy-start | bytes 28
  115.0 93.7 %all-to-all-start.2 = ((bf16[16,648,128]{2,1,0:T(8,128)(2,1)}), bf16[16,648,128]{2,1,0:T(8,128)(2,1)S(1)}, u32[]{:S(2)}, u32[]{:S(2)}) async-start(bf16[16,648,128]{2,1,0:T(8,128)(2,1)} %pad_maximum_fusion), calls=%async_computation.2 | async-start | bytes 5308416 | tf_op jit(solution)/shard_map/all_to_all | solution.py:185
  125.0 216.9 %reduce-scatter.2.cloned.1.call-start = ((), (), s32[]{:S(2)}) async-start(), calls=%async_computation.7 | async-start | bytes 3981312 | tf_op jit(solution)/shard_map/reduce_scatter | solution.py:215
  212.4 7.5 %copy-start.2 = (f32[1152,4608]{1,0:T(8,128)}, f32[1152,4608]{1,0:T(8,128)S(1)}, u32[]{:S(2)}) copy-start(f32[1152,4608]{1,0:T(8,128)S(1)} %get-tuple-element.37) | copy-start | bytes 63700996
  289.8 2.3 slice-start.1
  289.8 3.5 copy-start.4
  293.3 3.1 slice-start
  301.8 40.1 %copy-start.5 = (bf16[1,2,32,384]{3,2,1,0:T(8,128)(2,1)S(1)}, bf16[1,2,32,384]{3,2,1,0:T(8,128)(2,1)}, u32[]{:S(2)}) copy-start(bf16[1,2,32,384]{3,2,1,0:T(8,128)(2,1)} %param.12) | copy-start | bytes 147460
  301.8 48.1 %copy-start.1 = (bf16[192,3,384]{2,0,1:T(8,128)(2,1)S(1)}, bf16[192,3,384]{2,0,1:T(8,128)(2,1)}, u32[]{:S(2)}) copy-start(bf16[192,3,384]{2,0,1:T(8,128)(2,1)} %param.15) | copy-start | bytes 1327108
  343.1 5.8 %collective-permute-start = (bf16[1,256,384]{2,1,0:T(8,128)(2,1)S(1)}, bf16[1,256,384]{2,1,0:T(8,128)(2,1)S(1)}, u32[]{:S(2)}, u32[]{:S(2)}) collective-permute-start(bf16[1,256,384]{2,1,0:T(8,128)(2,1)S(1)} %constant_dynamic-slice_fusion), channel_id=1, source_target_pairs={{0,128},{128,0},{1,129},{129,1},{2,130},{130,2},{3,131},{131,3},{4... | collective-permute-start | bytes 589832 | tf_op jit(solution)/shard_map/ppermute | solution.py:226
Sparse Core Ops, SparseCore 0:
  11.0 81.1 all-gather.2
  94.6 195.1 all-gather.4
  301.9 39.9 reduce-scatter.1
